TPU v7x, 128 devices: a whole 4x4x4 slice. The times are simulated.
128 devices in a mesh: seq: 16 (over z, x), exp: 8 (over y, core).
Axes of the slice: x: 4, y: 4, z: 4, core: 2. Of those that a mesh axis runs over, the one named last changes fastest.
Arguments:
- residual_in: bfloat16 [8, 4096, 2048], P('exp', 'seq'), may hold values from -6 to 6
- query_matrix: bfloat16 [8, 4096, 2048], P('exp', 'seq'), may hold values from -6 to 6
- key_vectors: bfloat16 [8, 4096, 2048], P('exp', 'seq'), may hold values from -6 to 6
- value_vectors: bfloat16 [8, 4096, 2048], P('exp', 'seq'), may hold values from -6 to 6
- head_gain: float32 [2048], replicated, may hold values from 0.5 to 1.5
- norm_gain: float32 [2048], replicated, may hold values from 0.5 to 1.5
- expert_ids: int32 [8, 4096, 4], P('exp', 'seq'), may hold values from 0 to 7, all different within a row; in each aligned block of 256 rows (0 to 255, 256 to 511, ..., all dimensions but the last counted through in order) at most 192 rows name the same one
- gate_probs: float32 [8, 4096, 4], P('exp', 'seq'), may hold values from 0.25 to 1
- w_gate: bfloat16 [8, 2048, 1408], P('exp'), may hold values from -0.125 to 0.125
- w_up: bfloat16 [8, 2048, 1408], P('exp'), may hold values from -0.125 to 0.125
- w_down: bfloat16 [8, 1408, 2048], P('exp'), may hold values from -0.15625 to 0.15625
Outputs:
- layer_out: bfloat16 [8, 4096, 2048], P('exp', 'seq')
Inputs may be any that keep to these rules, and one draw needn't show every extreme that they name: `expert_ids`: the 4 experts of one position differ; among the 256 positions of one device, no expert is named by more than 192 routes.
All inputs are finite; a program needn't handle non-finite values.
Results may differ from a plain program's by a relative error of at most 0.013.
Values may be sent and summed in bfloat16 or wider, within the bound.
No kernel may reach another device: no remote copies, remote signals or barrier semaphores. Data moves between devices by JAX's collectives and lax.ppermute only.
A program may use at most 128 MiB of HBM per device.

v0:
```python
import jax
import jax.numpy as jnp
from jax import lax
from jax.sharding import PartitionSpec as P

D = 2048
HEADS = 16
HD = 128
TOP = 4
EXPERTS = 8
CHUNKS = 2


def block_prefix(state):
    blocks = lax.axis_size("seq")
    pieces = state.reshape(blocks, -1)
    gathered = lax.all_to_all(pieces, "seq", split_axis=0, concat_axis=0, tiled=True)
    shifted = jnp.concatenate([jnp.zeros_like(gathered[:1]), gathered[:-1]], axis=0)
    prefixes = lax.cumsum(shifted, axis=0).astype(jnp.bfloat16)
    mine = lax.all_to_all(prefixes, "seq", split_axis=0, concat_axis=0, tiled=True)
    return mine.reshape(state.shape)


def on_device(
    residual_in,
    query_matrix,
    key_vectors,
    value_vectors,
    head_gain,
    norm_gain,
    expert_ids,
    gate_probs,
    w_gate,
    w_up,
    w_down,
):
    positions = residual_in.shape[1]
    queries = query_matrix[0].reshape(positions, HEADS, HD)
    key_rows = key_vectors[0].reshape(positions, HEADS, HD)
    value_rows = value_vectors[0].reshape(positions, HEADS, HD)
    state = jnp.einsum("thd,the->hde", key_rows, value_rows, preferred_element_type=jnp.float32)
    prefix = block_prefix(state)
    causal = jnp.tril(jnp.ones((positions, positions), dtype=bool))
    scores = jnp.einsum("thd,uhd->htu", queries, key_rows, preferred_element_type=jnp.float32)
    weights = jnp.where(causal[None], scores, 0.0).astype(jnp.bfloat16)
    inner = jnp.einsum("htu,uhd->thd", weights, value_rows, preferred_element_type=jnp.float32)
    outer_product = jnp.einsum("thd,hde->the", queries, prefix, preferred_element_type=jnp.float32)
    mixed = inner + outer_product
    mean_square = jnp.mean(mixed * mixed, axis=-1, keepdims=True)
    attn = (mixed * lax.rsqrt(mean_square + 1e-06)).reshape(positions, D) * head_gain
    resid_float = (
        (residual_in[0].astype(jnp.float32) + attn).astype(jnp.bfloat16).astype(jnp.float32)
    )
    row_square = jnp.mean(resid_float * resid_float, axis=-1, keepdims=True)
    normed = (resid_float * lax.rsqrt(row_square + 1e-06) * norm_gain).astype(jnp.bfloat16)
    route_ids = expert_ids[0]
    route_gates = gate_probs[0]
    experts = jnp.arange(EXPERTS, dtype=jnp.int32)
    table = jnp.sum(
        jnp.where(route_ids[:, :, None] == experts[None, None, :], route_gates[:, :, None], 0.0),
        axis=1,
    )
    groups = lax.axis_size("exp")
    me = lax.axis_index("exp")
    local_count = w_gate.shape[0]
    high = table.astype(jnp.bfloat16)
    rest = table - high.astype(jnp.float32)
    middle = rest.astype(jnp.bfloat16)
    low = (rest - middle.astype(jnp.float32)).astype(jnp.bfloat16)
    pad = jnp.zeros((positions, 128 - 3 * EXPERTS), jnp.bfloat16)
    payload = jnp.concatenate([normed, high, middle, low, pad], axis=1)
    chunk = positions // CHUNKS
    outs = []
    for c in range(CHUNKS):
        gathered = lax.all_gather(payload[c * chunk : (c + 1) * chunk], "exp", axis=0, tiled=True)
        rows = gathered[:, :D]
        code = gathered[:, D : D + 3 * EXPERTS].astype(jnp.float32)
        code = lax.dynamic_slice_in_dim(
            code.reshape(-1, 3, EXPERTS), me * local_count, local_count, axis=2
        )
        weight = code[:, 0] + code[:, 1] + code[:, 2]
        gate_part = jnp.einsum("nd,edf->enf", rows, w_gate, preferred_element_type=jnp.float32)
        up_part = jnp.einsum("nd,edf->enf", rows, w_up, preferred_element_type=jnp.float32)
        hidden = (jax.nn.silu(gate_part) * up_part).astype(jnp.bfloat16)
        result = jnp.einsum("enf,efd->end", hidden, w_down, preferred_element_type=jnp.float32)
        result = result.astype(jnp.bfloat16).astype(jnp.float32)
        contrib = jnp.sum(result * weight.T[:, :, None], axis=0).astype(jnp.bfloat16)
        outs.append(lax.psum_scatter(contrib, "exp", scatter_dimension=0, tiled=True))
    combined = jnp.concatenate(outs, axis=0)
    return (resid_float + combined.astype(jnp.float32)).astype(jnp.bfloat16)[None]


def solution(mesh):
    in_specs = (
        P("exp", "seq", None),
        P("exp", "seq", None),
        P("exp", "seq", None),
        P("exp", "seq", None),
        P(),
        P(),
        P("exp", "seq", None),
        P("exp", "seq", None),
        P("exp", None, None),
        P("exp", None, None),
        P("exp", None, None),
    )
    out_specs = P("exp", "seq", None)
    return jax.shard_map(
        on_device, mesh=mesh, in_specs=in_specs, out_specs=out_specs, check_vma=False
    )
```

profile of v0, /device:TPU:0, one launch (start us, length us, event | category | flops | bytes accessed | tf_op | source)
XLA Modules:
  0.0 271.2 jit_solution(12462219032883238043)
XLA Ops:
  6.5 1.5 copy.77
  8.0 1.5 copy.79
  9.5 0.5 fusion.62
  10.0 0.0 copy-start.3
  10.0 0.0 copy-start.4
  10.0 24.9 %all_to_all.15 = f32[16,1,16384]{2,1,0:T(1,128)S(1)} all-to-all(f32[16,1,16384]{2,1,0:T(1,128)S(1)} %bitcast.158), channel_id=1, replica_groups=mesh['seq'=16,'exp'=8] {'seq'}, dimensions={0} | all-to-all | bytes 2097152 | tf_op jit(solution)/shard_map/all_to_all | solution.py:17
  34.9 0.7 reduce-window_convert_fusion
  35.6 0.6 broadcast.54
  36.2 4.6 %reduce.1 = bf16[16,16384]{1,0:T(8,128)(2,1)} reduce(bf16[16,1,16384]{2,1,0:T(2,128)(2,1)S(1)} %reduce-window_convert_fusion, bf16[]{:T(256)} %broadcast.54), dimensions={1}, to_apply=%reduce-window_convert_fusion.reduce_sub_computation | reduce | bytes 1048578 | tf_op jit(solution)/shard_map/block_prefix/reduce_window_sum | solution.py:19
  40.8 2.2 reshape.234
  43.1 4.2 %all-to-all-start.1 = ((bf16[16,2,8192]{2,1,0:T(2,128)(2,1)}), bf16[16,2,8192]{2,1,0:T(2,128)(2,1)}, u32[]{:S(2)}, u32[]{:S(2)}) async-start(bf16[16,2,8192]{2,1,0:T(2,128)(2,1)} %reshape.234), calls=%async_computation.1 | async-start | bytes 1048576 | tf_op jit(solution)/shard_map/all_to_all | solution.py:20
  47.3 0.2 all-gather.5.cloned.1.call-start
  47.6 0.0 copy-done.3
  47.6 1.5 copy.60
  49.1 2.4 copy.78
  51.5 4.0 %fusion.58 = f32[16,256,128]{1,2,0:T(8,128)} fusion(bf16[256,16,128]{0,2,1:T(8,128)(2,1)S(1)} %bitcast.155, pred[256,256]{1,0:T(8,128)(4,1)S(1)} %iota_compare_fusion, bf16[256,16,128]{2,1,0:T(8,128)(2,1)S(1)} %bitcast.157, bf16[256,16,128]{2,1,0:T(8,128)(2,1)} %bitcast.159), kind=kOutput, calls=%fused_computation.53 | convolution fusion | flops 538968064 | bytes 5308416 | tf_op jit(solution)/shard_map/htu,uhd->thd/dot_general | solution.py:46
  55.5 2.3 all-to-all-done.1
  57.8 2.2 reshape.235
  60.0 3.9 %reduce = bf16[16,16384]{1,0:T(8,128)(2,1)} reduce(bf16[16,1,16384]{2,1,0:T(2,128)(2,1)S(1)} %reshape.235, bf16[]{:T(256)} %constant.40), dimensions={1}, to_apply=%all_to_all.12.reduce_sub_computation | reduce | bytes 1048578 | tf_op jit(solution)/shard_map/all_to_all | solution.py:20
  64.0 1.1 copy.80
  65.1 0.0 copy-start.1
  65.1 2.2 multiply_reduce_fusion
  67.3 0.0 copy-start.2
  67.3 0.2 broadcast_multiply_fusion
  67.6 0.5 fusion.55
  68.1 0.3 fusion.59
  68.5 1.1 fusion.72
  69.5 0.0 all-gather.5.cloned.1.call-update
  69.6 0.0 all-gather.3.cloned.1.call-start
  69.6 0.7 all-gather.3.cloned.1.call-update
  70.3 0.3 reduce-scatter.9.cloned.1.call-start
  70.6 35.1 %all-gather.5.cloned.1.call-done = bf16[1024,2176]{0,1:T(8,128)(2,1)} async-done(((bf16[128,2176]{0,1:T(8,128)(2,1)}), bf16[1024,2176]{0,1:T(8,128)(2,1)}) %all-gather.5.cloned.1.call-update) | async-done | bytes 4456464 | tf_op jit(solution)/shard_map/all_gather | solution.py:75
  105.7 0.8 slice_bitcast_fusion
  106.5 38.5 %all-gather.3.cloned.1.call-done = bf16[1024,2176]{0,1:T(8,128)(2,1)} async-done(((bf16[128,2176]{0,1:T(8,128)(2,1)}), bf16[1024,2176]{0,1:T(8,128)(2,1)}) %all-gather.3.cloned.1.call-update) | async-done | bytes 4456464 | tf_op jit(solution)/shard_map/all_gather | solution.py:75
  145.0 0.8 slice_bitcast_fusion.1
  145.8 11.8 %fusion.9 = f32[1024,1408]{1,0:T(8,128)} fusion(bf16[1,2048,1408]{2,1,0:T(8,128)(2,1)} %param.20, bf16[1024,2176]{0,1:T(8,128)(2,1)} %all-gather.5.cloned.1.call-done), kind=kOutput, calls=%fused_computation.16 | convolution fusion | flops 5905580032 | bytes 15728640 | tf_op jit(solution)/shard_map/nd,edf->enf/dot_general | solution.py:83
  157.7 21.5 %multiply_convert_fusion = bf16[1024,2048]{1,0:T(8,128)(2,1)} fusion(f32[1024]{0:T(1024)S(1)} %bitcast.169, bf16[1,1408,2048]{2,1,0:T(8,128)(2,1)} %param.21, f32[1024,1408]{1,0:T(8,128)} %fusion.9, bf16[1,2048,1408]{2,1,0:T(8,128)(2,1)} %param.19, bf16[1024,2176]{0,1:T(8,128)(2,1)} %all-gather.5.cloned.1.call-done), kind=kOutput, calls=%fused_computation.1 | convolution fusion | flops 11828199424 | bytes 25694208 | tf_op jit(solution)/shard_map/enf,efd->end/dot_general | solution.py:85
  179.1 0.0 reduce-scatter.9.cloned.1.call-update
  179.2 0.3 reduce-scatter.7.cloned.1.call-start
  179.5 11.8 %fusion.11 = f32[1024,1408]{1,0:T(8,128)} fusion(bf16[1,2048,1408]{2,1,0:T(8,128)(2,1)} %param.20, bf16[1024,2176]{0,1:T(8,128)(2,1)} %all-gather.3.cloned.1.call-done), kind=kOutput, calls=%fused_computation.18 | convolution fusion | flops 5905580032 | bytes 15728640 | tf_op jit(solution)/shard_map/nd,edf->enf/dot_general | solution.py:83
  191.3 21.8 %multiply_convert_fusion.1 = bf16[1024,2048]{1,0:T(8,128)(2,1)} fusion(f32[1024]{0:T(1024)S(1)} %bitcast.170, bf16[1,1408,2048]{2,1,0:T(8,128)(2,1)} %param.21, f32[1024,1408]{1,0:T(8,128)} %fusion.11, bf16[1,2048,1408]{2,1,0:T(8,128)(2,1)} %param.19, bf16[1024,2176]{0,1:T(8,128)(2,1)} %all-gather.3.cloned.1.call-done), kind=kOutput, calls=%fused_computation.2 | convolution fusion | flops 11828199424 | bytes 25694208 | tf_op jit(solution)/shard_map/enf,efd->end/dot_general | solution.py:85
  213.1 0.0 reduce-scatter.7.cloned.1.call-update
  213.1 5.1 %reduce-scatter.9.cloned.1.call-done = bf16[128,2048]{1,0:T(8,128)(2,1)} async-done(((bf16[1024,2048]{1,0:T(8,128)(2,1)}), bf16[128,2048]{1,0:T(8,128)(2,1)}) %reduce-scatter.9.cloned.1.call-update) | async-done | bytes 524304
  218.2 2.0 copy.76
  220.3 37.1 %reduce-scatter.7.cloned.1.call-done = bf16[128,2048]{1,0:T(8,128)(2,1)} async-done(((bf16[1024,2048]{1,0:T(8,128)(2,1)}), bf16[128,2048]{1,0:T(8,128)(2,1)}) %reduce-scatter.7.cloned.1.call-update) | async-done | bytes 524304
  257.4 2.1 copy.74
  259.4 3.0 %add_convert_fusion = bf16[1,256,2048]{1,2,0:T(8,128)(2,1)} fusion(f32[256,16,128]{0,2,1:T(8,128)S(1)} %broadcast_multiply_fusion, bf16[1,256,2048]{1,2,0:T(8,128)(2,1)S(1)} %copy.60, bf16[1,128,2048]{1,2,0:T(8,128)(2,1)} %bitcast.161, bf16[1,128,2048]{1,2,0:T(8,128)(2,1)} %bitcast.162, f32[2048]{0:T(1024)S(1)} %copy-done.1), kind=kLoop, calls=%fused_computation.51 | loop fusion | flops 5767168 | bytes 5251072 | tf_op jit(solution)/shard_map/convert_element_type | solution.py:90
  262.4 2.3 copy.71
  (16 shorter events, 0.1 us)
Async XLA Ops:
  10.0 37.6 %copy-start.3 = (f32[1,256,4]{1,2,0:T(4,128)S(1)}, f32[1,256,4]{1,2,0:T(4,128)}, u32[]{:S(2)}) copy-start(f32[1,256,4]{1,2,0:T(4,128)} %param.18) | copy-start | bytes 12292
  10.0 37.6 %copy-start.4 = (s32[1,256,4]{1,2,0:T(4,128)S(1)}, s32[1,256,4]{1,2,0:T(4,128)}, u32[]{:S(2)}) copy-start(s32[1,256,4]{1,2,0:T(4,128)} %param.17) | copy-start | bytes 12292
  43.1 14.7 %all-to-all-start.1 = ((bf16[16,2,8192]{2,1,0:T(2,128)(2,1)}), bf16[16,2,8192]{2,1,0:T(2,128)(2,1)}, u32[]{:S(2)}, u32[]{:S(2)}) async-start(bf16[16,2,8192]{2,1,0:T(2,128)(2,1)} %reshape.234), calls=%async_computation.1 | async-start | bytes 1048576 | tf_op jit(solution)/shard_map/all_to_all | solution.py:20
  47.3 58.4 %all-gather.5.cloned.1.call-start = ((), (), s32[]{:S(2)}) async-start(), calls=%async_computation.5 | async-start | bytes 5013504 | tf_op jit(solution)/shard_map/all_gather | solution.py:75
  55.5 9.6 %copy-start = (bf16[32,8,16,128]{3,2,1,0:T(8,128)(2,1)S(1)}, bf16[32,8,16,128]{3,2,1,0:T(8,128)(2,1)}, u32[]{:S(2)}) copy-start(bf16[32,8,16,128]{3,2,1,0:T(8,128)(2,1)} %copy.78) | copy-start | bytes 3145732
  65.1 2.5 copy-start.1
  67.3 0.7 copy-start.2
  69.6 75.4 %all-gather.3.cloned.1.call-start = ((), (), s32[]{:S(2)}) async-start(), calls=%async_computation.4 | async-start | bytes 5013504 | tf_op jit(solution)/shard_map/all_gather | solution.py:75
  70.3 147.9 %reduce-scatter.9.cloned.1.call-start = ((), (), s32[]{:S(2)}) async-start(), calls=%async_computation.7 | async-start | bytes 4718592
  179.2 78.2 %reduce-scatter.7.cloned.1.call-start = ((), (), s32[]{:S(2)}) async-start(), calls=%async_computation.6 | async-start | bytes 4718592
Sparse Core Ops, SparseCore 0:
  69.7 36.0 all-gather.4
  107.4 37.5 all-gather.2
  179.3 38.9 reduce-scatter.8
  220.5 36.8 reduce-scatter.6
where the time goes:
time: 272 us; the launch traced here: 271 us
  waiting for transfers between devices  119 us (44%)
  matrix products  73.5 us (27%)
  blocking collectives  24.9 us (9%)
  local copies, waits for them, and re-layouts  22.1 us (8%)
  other arithmetic  13.4 us (5%)
  between operations  13.4 us (5%)
  starting transfers between devices  5.06 us (2%)
    all_gather x2, waiting for transfers between devices, on_device(): lax.all_gather(payload[c * chunk:(c + 1) * chunk], 'exp', axis=0, tiled=T...  73.6 us
    dot_general x2, matrix products, on_device(): jnp.einsum('enf,efd->end', hidden, w_down, preferred_element_type=jnp.flo...  43.2 us
    unnamed x6, waiting for transfers between devices  43 us
    all_to_all x1, blocking collectives, block_prefix(): lax.all_to_all(pieces, 'seq', split_axis=0, concat_axis=0, tiled=True)  24.9 us
    dot_general x2, matrix products, on_device(): jnp.einsum('nd,edf->enf', rows, w_up, preferred_element_type=jnp.float32)  23.7 us
    unnamed x20, local copies, waits for them, and re-layouts  16.7 us
  transfers between devices with their start and end apart: 5, of which 5 were waited for; matrix products, arithmetic and copies ran while one was open for 16% of the time, Pallas kernels for 0%

commit v1 on v0

--- a/solution.py
+++ b/solution.py
@@ -9,6 +9,35 @@
 TOP = 4
 EXPERTS = 8
 CHUNKS = 2
+
+
+def perform_weights(mine_x):
+    local_out = lax.axis_size("exp")
+    upper = lax.axis_index("exp")
+    left_arr, parts_out, aux = (local_out, upper, mine_x.shape[0])
+    views = []
+    for nth, k in enumerate(mine_x.shape):
+        views.append(k * left_arr if nth == 0 else k)
+    mat_out = jnp.zeros(views, mine_x.dtype)
+    then = lax.dynamic_update_slice_in_dim(mat_out, mine_x, parts_out * aux, axis=0)
+    f_next = all_values = mine_x
+    for src_i in range(1, left_arr // 2 + 1):
+        items = []
+        for nth in range(left_arr):
+            items.append((nth, (nth + 1) % left_arr))
+        f_next = lax.ppermute(f_next, "exp", items)
+        then = lax.dynamic_update_slice_in_dim(
+            then, f_next, (parts_out - src_i) % left_arr * aux, axis=0
+        )
+        if 2 * src_i < left_arr:
+            row_list = []
+            for nth in range(left_arr):
+                row_list.append((nth, (nth - 1) % left_arr))
+            all_values = lax.ppermute(all_values, "exp", row_list)
+            then = lax.dynamic_update_slice_in_dim(
+                then, all_values, (parts_out + src_i) % left_arr * aux, axis=0
+            )
+    return then
 
 
 def block_prefix(state):
@@ -72,7 +101,7 @@
     chunk = positions // CHUNKS
     outs = []
     for c in range(CHUNKS):
-        gathered = lax.all_gather(payload[c * chunk : (c + 1) * chunk], "exp", axis=0, tiled=True)
+        gathered = perform_weights(payload[c * chunk : (c + 1) * chunk])
         rows = gathered[:, :D]
         code = gathered[:, D : D + 3 * EXPERTS].astype(jnp.float32)
         code = lax.dynamic_slice_in_dim(

time: 272 us -> 269 us (0.989)
  waiting for transfers between devices: 119 us -> 72.8 us
  local copies, waits for them, and re-layouts: 22.1 us -> 65.5 us
  blocking collectives: 24.9 us -> 0 us
  starting transfers between devices: 5.06 us -> 24.9 us
  other arithmetic: 13.4 us -> 16.6 us
    all_gather x2 -> x0, waiting for transfers between devices: 73.6 us -> none  [on_device(): lax.all_gather(payload[c * chunk:(c + 1) * chunk], 'exp', axis=0, tiled=T...]
    unnamed x6 -> x2, waiting for transfers between devices: 43 us -> 0.03 us
    reduce_scatter x0 -> x2, waiting for transfers between devices: none -> 36.9 us  [on_device(): lax.psum_scatter(contrib, 'exp', scatter_dimension=0, tiled=True)]
    all_to_all x1 -> x0, blocking collectives: 24.9 us -> none  [block_prefix(): lax.all_to_all(pieces, 'seq', split_axis=0, concat_axis=0, tiled=True)]
    ppermute x0 -> x14, local copies, waits for them, and re-layouts: none -> 21.2 us  [the longest x8 13 us: perform_weights(): f_next = lax.ppermute(f_next, 'exp', items)]
    all_to_all x0 -> x1, waiting for transfers between devices: none -> 17.7 us  [block_prefix(): lax.all_to_all(pieces, 'seq', split_axis=0, concat_axis=0, tiled=True)]
    dynamic_update_slice x0 -> x16, local copies, waits for them, and re-layouts: none -> 17.6 us  [the longest x8 10.3 us: perform_weights(): lax.dynamic_update_slice_in_dim(then, f_next, (parts_out - src_i) % left_...]
    ppermute x0 -> x14, waiting for transfers between devices: none -> 12.9 us  [the longest x8 12.9 us: perform_weights(): f_next = lax.ppermute(f_next, 'exp', items)]
  transfers between devices with their start and end apart: 5 -> 18, of which waited for: 5 -> 6; matrix products, arithmetic and copies ran while one was open for 16% -> 32% of each run, Pallas kernels for 0% -> 0%
where the time goes in v1:
time: 269 us; the launch traced here: 267 us
  matrix products  73.4 us (27%)
  waiting for transfers between devices  72.8 us (27%)
  local copies, waits for them, and re-layouts  65.5 us (24%)
  starting transfers between devices  24.9 us (9%)
  other arithmetic  16.6 us (6%)
  between operations  13.9 us (5%)
    dot_general x2, matrix products, on_device(): jnp.einsum('enf,efd->end', hidden, w_down, preferred_element_type=jnp.flo...  42.8 us
    reduce_scatter x2, waiting for transfers between devices, on_device(): lax.psum_scatter(contrib, 'exp', scatter_dimension=0, tiled=True)  36.9 us
    dot_general x2, matrix products, on_device(): jnp.einsum('nd,edf->enf', rows, w_gate, preferred_element_type=jnp.float32)  24.3 us
    all_to_all x1, waiting for transfers between devices, block_prefix(): lax.all_to_all(pieces, 'seq', split_axis=0, concat_axis=0, tiled=True)  17.7 us
    ppermute x8, local copies, waits for them, and re-layouts, perform_weights(): f_next = lax.ppermute(f_next, 'exp', items)  13 us
    ppermute x8, waiting for transfers between devices, perform_weights(): f_next = lax.ppermute(f_next, 'exp', items)  12.9 us
    ppermute x6, starting transfers between devices, perform_weights(): all_values = lax.ppermute(all_values, 'exp', row_list)  11.5 us
    dynamic_update_slice x8, local copies, waits for them, and re-layouts, perform_weights(): lax.dynamic_update_slice_in_dim(then, f_next, (parts_out - src_i) % left_...  10.3 us
  transfers between devices with their start and end apart: 18, of which 6 were waited for; matrix products, arithmetic and copies ran while one was open for 32% of the time, Pallas kernels for 0%

profile of v1, /device:TPU:0, one launch (start us, length us, event | category | flops | bytes accessed | tf_op | source)
XLA Modules:
  0.0 267.0 jit_solution(11494167517751052896)
XLA Ops:
  6.5 1.5 copy.106
  8.0 1.5 copy.108
  9.5 1.4 fusion.61
  11.0 8.0 %all-to-all-start = ((f32[16,1,16384]{2,1,0:T(1,128)}), f32[16,1,16384]{2,1,0:T(1,128)}, u32[]{:S(2)}, u32[]{:S(2)}) async-start(f32[16,1,16384]{2,1,0:T(1,128)} %bitcast.1), calls=%async_computation | async-start | bytes 2097152 | tf_op jit(solution)/shard_map/all_to_all | solution.py:46
  19.0 17.7 %all-to-all-done = f32[16,1,16384]{2,1,0:T(1,128)} async-done(((f32[16,1,16384]{2,1,0:T(1,128)}), f32[16,1,16384]{2,1,0:T(1,128)}, u32[]{:S(2)}, u32[]{:S(2)}) %all-to-all-start) | async-done | bytes 1048608 | tf_op jit(solution)/shard_map/all_to_all | solution.py:46
  36.7 1.9 reduce-window_convert_fusion
  39.2 4.6 %reduce.1 = bf16[16,16384]{1,0:T(8,128)(2,1)} reduce(bf16[16,1,16384]{2,1,0:T(2,128)(2,1)S(1)} %reduce-window_convert_fusion, bf16[]{:T(256)} %broadcast.65), dimensions={1}, to_apply=%reduce-window_convert_fusion.reduce_sub_computation | reduce | bytes 1048578 | tf_op jit(solution)/shard_map/block_prefix/reduce_window_sum | solution.py:48
  43.8 2.2 reshape.230
  46.0 4.2 %all-to-all-start.1 = ((bf16[16,2,8192]{2,1,0:T(2,128)(2,1)}), bf16[16,2,8192]{2,1,0:T(2,128)(2,1)}, u32[]{:S(2)}, u32[]{:S(2)}) async-start(bf16[16,2,8192]{2,1,0:T(2,128)(2,1)} %reshape.230), calls=%async_computation.1 | async-start | bytes 1048576 | tf_op jit(solution)/shard_map/all_to_all | solution.py:49
  50.8 1.4 copy.107
  52.3 2.7 %fusion.58 = f32[16,256,128]{1,2,0:T(8,128)} fusion(bf16[256,16,128]{0,2,1:T(8,128)(2,1)S(1)} %bitcast.146, pred[256,256]{1,0:T(8,128)(4,1)S(1)} %iota_compare_fusion, bf16[256,16,128]{2,1,0:T(8,128)(2,1)S(1)} %bitcast.148, bf16[256,16,128]{2,1,0:T(8,128)(2,1)S(1)} %bitcast.149), kind=kOutput, calls=%fused_computation.51 | convolution fusion | flops 538968064 | bytes 5308416 | tf_op jit(solution)/shard_map/htu,uhd->thd/dot_general | solution.py:75
  55.0 5.3 %all-to-all-done.1 = bf16[16,2,8192]{2,1,0:T(2,128)(2,1)} async-done(((bf16[16,2,8192]{2,1,0:T(2,128)(2,1)}), bf16[16,2,8192]{2,1,0:T(2,128)(2,1)}, u32[]{:S(2)}, u32[]{:S(2)}) %all-to-all-start.1) | async-done | bytes 524320 | tf_op jit(solution)/shard_map/all_to_all | solution.py:49
  60.3 2.2 reshape.231
  62.6 3.1 %reduce = bf16[16,16384]{1,0:T(8,128)(2,1)S(1)} reduce(bf16[16,1,16384]{2,1,0:T(2,128)(2,1)S(1)} %reshape.231, bf16[]{:T(256)} %constant.108), dimensions={1}, to_apply=%all_to_all.12.reduce_sub_computation | reduce | bytes 1048578 | tf_op jit(solution)/shard_map/all_to_all | solution.py:49
  65.8 2.2 multiply_reduce_fusion
  68.3 1.8 copy.85
  70.2 2.1 fusion.55
  73.6 2.4 concatenate.18
  80.2 2.6 collective-permute-start.8
  82.9 2.7 broadcast.63.clone
  86.5 2.7 %broadcast.63.clone.1 = bf16[1024,2176]{0,1:T(8,128)(2,1)} broadcast(bf16[]{:T(256)} %constant.83.clone.1), dimensions={} | broadcast | bytes 4456450 | tf_op jit(solution)/shard_map/broadcast.3
  90.1 1.4 copy.91
  91.4 3.0 %collective-permute-start.3 = (bf16[128,2176]{1,0:T(8,128)(2,1)}, bf16[128,2176]{1,0:T(8,128)(2,1)}, u32[]{:S(2)}, u32[]{:S(2)}) collective-permute-start(bf16[128,2176]{1,0:T(8,128)(2,1)} %collective-permute-done.1), channel_id=1, source_target_pairs={{0,7},{1,0},{2,1},{3,2},{4,3},{5,4},{6,5},{7,6},{8,15},{9,8},{10,9... | collective-permute-start | bytes 1671176 | tf_op jit(solution)/shard_map/ppermute | solution.py:36
  94.4 1.4 copy.90
  95.8 2.1 copy.98
  97.9 2.0 constant_dynamic-update-slice_fusion.6
  100.8 1.4 copy.99
  102.1 2.9 %collective-permute-start.10 = (bf16[128,2176]{1,0:T(8,128)(2,1)}, bf16[128,2176]{1,0:T(8,128)(2,1)}, u32[]{:S(2)}, u32[]{:S(2)}) collective-permute-start(bf16[128,2176]{1,0:T(8,128)(2,1)} %collective-permute-done.8), channel_id=1, source_target_pairs={{0,7},{1,0},{2,1},{3,2},{4,3},{5,4},{6,5},{7,6},{8,15},{9,8},{10,9... | collective-permute-start | bytes 1671176 | tf_op jit(solution)/shard_map/ppermute | solution.py:36
  106.8 1.4 copy.93
  108.2 3.0 %collective-permute-start.5 = (bf16[128,2176]{1,0:T(8,128)(2,1)}, bf16[128,2176]{1,0:T(8,128)(2,1)}, u32[]{:S(2)}, u32[]{:S(2)}) collective-permute-start(bf16[128,2176]{1,0:T(8,128)(2,1)} %collective-permute-done.3), channel_id=1, source_target_pairs={{0,7},{1,0},{2,1},{3,2},{4,3},{5,4},{6,5},{7,6},{8,15},{9,8},{10,9... | collective-permute-start | bytes 1671176 | tf_op jit(solution)/shard_map/ppermute | solution.py:36
  111.2 1.4 copy.92
  112.5 3.0 %collective-permute-done.9 = bf16[128,2176]{1,0:T(8,128)(2,1)} collective-permute-done((bf16[128,2176]{1,0:T(8,128)(2,1)}, bf16[128,2176]{1,0:T(8,128)(2,1)}, u32[]{:S(2)}, u32[]{:S(2)}) %collective-permute-start.9) | collective-permute-done | bytes 557088 | tf_op jit(solution)/shard_map/ppermute | solution.py:28
  115.5 2.1 copy.100
  117.6 2.0 constant_dynamic-update-slice_fusion.4
  125.5 6.8 %collective-permute-done.11 = bf16[128,2176]{1,0:T(8,128)(2,1)} collective-permute-done((bf16[128,2176]{1,0:T(8,128)(2,1)}, bf16[128,2176]{1,0:T(8,128)(2,1)}, u32[]{:S(2)}, u32[]{:S(2)}) %collective-permute-start.11) | collective-permute-done | bytes 557088 | tf_op jit(solution)/shard_map/ppermute | solution.py:28
  132.3 2.1 copy.102
  134.4 1.4 copy.95
  135.8 2.0 constant_dynamic-update-slice_fusion.2
  138.6 1.4 copy.103
  141.7 3.1 %collective-permute-done.13 = bf16[128,2176]{1,0:T(8,128)(2,1)} collective-permute-done((bf16[128,2176]{1,0:T(8,128)(2,1)}, bf16[128,2176]{1,0:T(8,128)(2,1)}, u32[]{:S(2)}, u32[]{:S(2)}) %collective-permute-start.13) | collective-permute-done | bytes 557088 | tf_op jit(solution)/shard_map/ppermute | solution.py:28
  147.9 1.4 copy.96
  151.0 12.1 %fusion.18 = f32[1024,1408]{1,0:T(8,128)} fusion(bf16[1,2048,1408]{2,1,0:T(8,128)(2,1)} %param.19, bf16[1024,2176]{0,1:T(8,128)(2,1)} %constant_dynamic-update-slice_fusion.8), kind=kOutput, calls=%fused_computation.27 | convolution fusion | flops 5905580032 | bytes 15728640 | tf_op jit(solution)/shard_map/nd,edf->enf/dot_general | solution.py:111
  163.1 21.3 %multiply_convert_fusion.1 = bf16[1024,2048]{1,0:T(8,128)(2,1)} fusion(f32[1024]{0:T(1024)S(1)} %bitcast.159, bf16[1,1408,2048]{2,1,0:T(8,128)(2,1)} %param.21, bf16[1,2048,1408]{2,1,0:T(8,128)(2,1)} %param.20, bf16[1024,2176]{0,1:T(8,128)(2,1)} %constant_dynamic-update-slice_fusion.8, f32[1024,1408]{1,0:T(8,128)} %fusion.18), kind=kOutput, calls=%fused_computation.2 | convolution fusion | flops 11828199424 | bytes 25694208 | tf_op jit(solution)/shard_map/enf,efd->end/dot_general | solution.py:114
  184.5 12.2 %fusion.16 = f32[1024,1408]{1,0:T(8,128)} fusion(bf16[1,2048,1408]{2,1,0:T(8,128)(2,1)} %param.19, bf16[1024,2176]{0,1:T(8,128)(2,1)} %constant_dynamic-update-slice_fusion), kind=kOutput, calls=%fused_computation.25 | convolution fusion | flops 5905580032 | bytes 15728640 | tf_op jit(solution)/shard_map/nd,edf->enf/dot_general | solution.py:111
  196.6 21.5 %multiply_convert_fusion = bf16[1024,2048]{1,0:T(8,128)(2,1)} fusion(f32[1024]{0:T(1024)S(1)} %bitcast.160, bf16[1,1408,2048]{2,1,0:T(8,128)(2,1)} %param.21, bf16[1,2048,1408]{2,1,0:T(8,128)(2,1)} %param.20, bf16[1024,2176]{0,1:T(8,128)(2,1)} %constant_dynamic-update-slice_fusion, f32[1024,1408]{1,0:T(8,128)} %fusion.16), kind=kOutput, calls=%fused_computation.1 | convolution fusion | flops 11828199424 | bytes 25694208 | tf_op jit(solution)/shard_map/enf,efd->end/dot_general | solution.py:114
  218.2 1.8 copy.84
  220.0 36.9 %reduce-scatter.5.cloned.1.call-done = bf16[128,2048]{1,0:T(8,128)(2,1)} async-done(((bf16[1024,2048]{1,0:T(8,128)(2,1)}), bf16[128,2048]{1,0:T(8,128)(2,1)}) %reduce-scatter.5.cloned.1.call-update) | async-done | bytes 524304 | tf_op jit(solution)/shard_map/reduce_scatter | solution.py:117
  256.9 3.3 %add_convert_fusion = bf16[1,256,2048]{2,1,0:T(8,128)(2,1)} fusion(f32[1,256,2048]{2,1,0:T(8,128)} %copy.84, bf16[1,256,2048]{2,1,0:T(8,128)(2,1)S(1)} %copy-done.1, bf16[1,128,2048]{2,1,0:T(8,128)(2,1)} %bitcast.156, bf16[1,128,2048]{2,1,0:T(8,128)(2,1)} %bitcast.155, f32[2048]{0:T(1024)S(1)} %copy-done.2), kind=kLoop, calls=%fused_computation.49 | loop fusion | flops 5767168 | bytes 5251072 | tf_op jit(solution)/shard_map/convert_element_type | solution.py:119
  (75 shorter events, 25.0 us)
Async XLA Ops:
  6.5 12.5 %copy-start.4 = (f32[1,256,4]{1,2,0:T(4,128)S(1)}, f32[1,256,4]{1,2,0:T(4,128)}, u32[]{:S(2)}) copy-start(f32[1,256,4]{1,2,0:T(4,128)} %param.18) | copy-start | bytes 12292
  6.5 12.5 %copy-start.5 = (s32[1,256,4]{1,2,0:T(4,128)S(1)}, s32[1,256,4]{1,2,0:T(4,128)}, u32[]{:S(2)}) copy-start(s32[1,256,4]{1,2,0:T(4,128)} %param.17) | copy-start | bytes 12292
  11.0 25.8 %all-to-all-start = ((f32[16,1,16384]{2,1,0:T(1,128)}), f32[16,1,16384]{2,1,0:T(1,128)}, u32[]{:S(2)}, u32[]{:S(2)}) async-start(f32[16,1,16384]{2,1,0:T(1,128)} %bitcast.1), calls=%async_computation | async-start | bytes 2097152 | tf_op jit(solution)/shard_map/all_to_all | solution.py:46
  46.0 14.3 %all-to-all-start.1 = ((bf16[16,2,8192]{2,1,0:T(2,128)(2,1)}), bf16[16,2,8192]{2,1,0:T(2,128)(2,1)}, u32[]{:S(2)}, u32[]{:S(2)}) async-start(bf16[16,2,8192]{2,1,0:T(2,128)(2,1)} %reshape.230), calls=%async_computation.1 | async-start | bytes 1048576 | tf_op jit(solution)/shard_map/all_to_all | solution.py:49
  50.2 169.8 %reduce-scatter.3.cloned.1.call-start = ((), (), s32[]{:S(2)}) async-start(), calls=%async_computation.4 | async-start | bytes 4718592 | tf_op jit(solution)/shard_map/reduce_scatter | solution.py:117
  68.0 2.2 copy-start
  68.0 2.1 copy-start.2
  68.3 4.0 %copy-start.3 = (f32[2048]{0:T(1024)S(1)}, f32[2048]{0:T(1024)}, u32[]{:S(2)}) copy-start(f32[2048]{0:T(1024)} %param.16) | copy-start | bytes 24580
  78.4 11.7 %collective-permute-start.1 = (bf16[128,2176]{1,0:T(8,128)(2,1)}, bf16[128,2176]{1,0:T(8,128)(2,1)}, u32[]{:S(2)}, u32[]{:S(2)}) collective-permute-start(bf16[128,2176]{1,0:T(8,128)(2,1)} %get-tuple-element.7), channel_id=1, source_target_pairs={{0,7},{1,0},{2,1},{3,2},{4,3},{5,4},{6,5},{7,6},{8,15},{9,8},{10,9... | collective-permute-start | bytes 1671176 | tf_op jit(solution)/shard_map/ppermute | solution.py:36
  78.4 16.0 %collective-permute-start = (bf16[128,2176]{1,0:T(8,128)(2,1)}, bf16[128,2176]{1,0:T(8,128)(2,1)}, u32[]{:S(2)}, u32[]{:S(2)}) collective-permute-start(bf16[128,2176]{1,0:T(8,128)(2,1)} %get-tuple-element.7), channel_id=1, source_target_pairs={{0,1},{1,2},{2,3},{3,4},{4,5},{5,6},{6,7},{7,0},{8,9},{9,10},{10,1... | collective-permute-start | bytes 1671176 | tf_op jit(solution)/shard_map/ppermute | solution.py:28
  80.2 20.5 %collective-permute-start.8 = (bf16[128,2176]{1,0:T(8,128)(2,1)}, bf16[128,2176]{1,0:T(8,128)(2,1)}, u32[]{:S(2)}, u32[]{:S(2)}) collective-permute-start(bf16[128,2176]{1,0:T(8,128)(2,1)} %get-tuple-element.8), channel_id=1, source_target_pairs={{0,7},{1,0},{2,1},{3,2},{4,3},{5,4},{6,5},{7,6},{8,15},{9,8},{10,9... | collective-permute-start | bytes 1671176 | tf_op jit(solution)/shard_map/ppermute | solution.py:36
  82.9 12.9 %collective-permute-start.7 = (bf16[128,2176]{1,0:T(8,128)(2,1)}, bf16[128,2176]{1,0:T(8,128)(2,1)}, u32[]{:S(2)}, u32[]{:S(2)}) collective-permute-start(bf16[128,2176]{1,0:T(8,128)(2,1)} %get-tuple-element.8), channel_id=1, source_target_pairs={{0,1},{1,2},{2,3},{3,4},{4,5},{5,6},{6,7},{7,0},{8,9},{9,10},{10,1... | collective-permute-start | bytes 1671176 | tf_op jit(solution)/shard_map/ppermute | solution.py:28
  91.4 15.4 %collective-permute-start.3 = (bf16[128,2176]{1,0:T(8,128)(2,1)}, bf16[128,2176]{1,0:T(8,128)(2,1)}, u32[]{:S(2)}, u32[]{:S(2)}) collective-permute-start(bf16[128,2176]{1,0:T(8,128)(2,1)} %collective-permute-done.1), channel_id=1, source_target_pairs={{0,7},{1,0},{2,1},{3,2},{4,3},{5,4},{6,5},{7,6},{8,15},{9,8},{10,9... | collective-permute-start | bytes 1671176 | tf_op jit(solution)/shard_map/ppermute | solution.py:36
  95.8 15.4 %collective-permute-start.2 = (bf16[128,2176]{1,0:T(8,128)(2,1)}, bf16[128,2176]{1,0:T(8,128)(2,1)}, u32[]{:S(2)}, u32[]{:S(2)}) collective-permute-start(bf16[128,2176]{1,0:T(8,128)(2,1)} %collective-permute-done), channel_id=1, source_target_pairs={{0,1},{1,2},{2,3},{3,4},{4,5},{5,6},{6,7},{7,0},{8,9},{9,10},{10,1... | collective-permute-start | bytes 1671176 | tf_op jit(solution)/shard_map/ppermute | solution.py:28
  102.1 18.3 %collective-permute-start.10 = (bf16[128,2176]{1,0:T(8,128)(2,1)}, bf16[128,2176]{1,0:T(8,128)(2,1)}, u32[]{:S(2)}, u32[]{:S(2)}) collective-permute-start(bf16[128,2176]{1,0:T(8,128)(2,1)} %collective-permute-done.8), channel_id=1, source_target_pairs={{0,7},{1,0},{2,1},{3,2},{4,3},{5,4},{6,5},{7,6},{8,15},{9,8},{10,9... | collective-permute-start | bytes 1671176 | tf_op jit(solution)/shard_map/ppermute | solution.py:36
  105.0 10.5 %collective-permute-start.9 = (bf16[128,2176]{1,0:T(8,128)(2,1)}, bf16[128,2176]{1,0:T(8,128)(2,1)}, u32[]{:S(2)}, u32[]{:S(2)}) collective-permute-start(bf16[128,2176]{1,0:T(8,128)(2,1)} %collective-permute-done.7), channel_id=1, source_target_pairs={{0,1},{1,2},{2,3},{3,4},{4,5},{5,6},{6,7},{7,0},{8,9},{9,10},{10,1... | collective-permute-start | bytes 1671176 | tf_op jit(solution)/shard_map/ppermute | solution.py:28
  108.2 26.2 %collective-permute-start.5 = (bf16[128,2176]{1,0:T(8,128)(2,1)}, bf16[128,2176]{1,0:T(8,128)(2,1)}, u32[]{:S(2)}, u32[]{:S(2)}) collective-permute-start(bf16[128,2176]{1,0:T(8,128)(2,1)} %collective-permute-done.3), channel_id=1, source_target_pairs={{0,7},{1,0},{2,1},{3,2},{4,3},{5,4},{6,5},{7,6},{8,15},{9,8},{10,9... | collective-permute-start | bytes 1671176 | tf_op jit(solution)/shard_map/ppermute | solution.py:36
  112.5 11.6 %collective-permute-start.4 = (bf16[128,2176]{1,0:T(8,128)(2,1)}, bf16[128,2176]{1,0:T(8,128)(2,1)}, u32[]{:S(2)}, u32[]{:S(2)}) collective-permute-start(bf16[128,2176]{1,0:T(8,128)(2,1)} %collective-permute-done.2), channel_id=1, source_target_pairs={{0,1},{1,2},{2,3},{3,4},{4,5},{5,6},{6,7},{7,0},{8,9},{9,10},{10,1... | collective-permute-start | bytes 1671176 | tf_op jit(solution)/shard_map/ppermute | solution.py:28
  121.8 16.8 %collective-permute-start.12 = (bf16[128,2176]{1,0:T(8,128)(2,1)}, bf16[128,2176]{1,0:T(8,128)(2,1)}, u32[]{:S(2)}, u32[]{:S(2)}) collective-permute-start(bf16[128,2176]{1,0:T(8,128)(2,1)} %collective-permute-done.10), channel_id=1, source_target_pairs={{0,7},{1,0},{2,1},{3,2},{4,3},{5,4},{6,5},{7,6},{8,15},{9,8},{10,9... | collective-permute-start | bytes 1671176 | tf_op jit(solution)/shard_map/ppermute | solution.py:36
  121.8 10.5 %collective-permute-start.11 = (bf16[128,2176]{1,0:T(8,128)(2,1)}, bf16[128,2176]{1,0:T(8,128)(2,1)}, u32[]{:S(2)}, u32[]{:S(2)}) collective-permute-start(bf16[128,2176]{1,0:T(8,128)(2,1)} %collective-permute-done.9), channel_id=1, source_target_pairs={{0,1},{1,2},{2,3},{3,4},{4,5},{5,6},{6,7},{7,0},{8,9},{9,10},{10,1... | collective-permute-start | bytes 1671176 | tf_op jit(solution)/shard_map/ppermute | solution.py:28
  125.5 22.5 %collective-permute-start.6 = (bf16[128,2176]{1,0:T(8,128)(2,1)}, bf16[128,2176]{1,0:T(8,128)(2,1)}, u32[]{:S(2)}, u32[]{:S(2)}) collective-permute-start(bf16[128,2176]{1,0:T(8,128)(2,1)} %collective-permute-done.4), channel_id=1, source_target_pairs={{0,1},{1,2},{2,3},{3,4},{4,5},{5,6},{6,7},{7,0},{8,9},{9,10},{10,1... | collective-permute-start | bytes 1671176 | tf_op jit(solution)/shard_map/ppermute | solution.py:28
  134.4 10.5 %collective-permute-start.13 = (bf16[128,2176]{1,0:T(8,128)(2,1)}, bf16[128,2176]{1,0:T(8,128)(2,1)}, u32[]{:S(2)}, u32[]{:S(2)}) collective-permute-start(bf16[128,2176]{1,0:T(8,128)(2,1)} %collective-permute-done.11), channel_id=1, source_target_pairs={{0,1},{1,2},{2,3},{3,4},{4,5},{5,6},{6,7},{7,0},{8,9},{9,10},{10,1... | collective-permute-start | bytes 1671176 | tf_op jit(solution)/shard_map/ppermute | solution.py:28
  184.4 72.5 %reduce-scatter.5.cloned.1.call-start = ((), (), s32[]{:S(2)}) async-start(), calls=%async_computation.5 | async-start | bytes 4718592 | tf_op jit(solution)/shard_map/reduce_scatter | solution.py:117
  218.2 38.7 %copy-start.1 = (bf16[1,256,2048]{2,1,0:T(8,128)(2,1)S(1)}, bf16[1,256,2048]{2,1,0:T(8,128)(2,1)}, u32[]{:S(2)}) copy-start(bf16[1,256,2048]{2,1,0:T(8,128)(2,1)} %param.11) | copy-start | bytes 3145732
Sparse Core Ops, SparseCore 0:
  184.5 33.0 reduce-scatter.2
  220.0 36.8 reduce-scatter.4
